TPU v7x, 512 devices: a whole 4x4x16 slice. The times are simulated.
512 devices in a mesh: tm: 32 (over z, x_lo), recv: 16 (over x_hi, y, core).
Axes of the slice: x: 4 (x_hi: 2, x_lo: 2; x = x_hi * 2 + x_lo), y: 4, z: 16, core: 2. Of those that a mesh axis runs over, the one named last changes fastest.
Arguments:
- traces: bfloat16 [128, 4096, 2048], P('tm', 'recv'), may hold values from -6 to 6
- valid: int32 [128, 4096], P('tm', 'recv'), may hold values 0 or 1
- src_idx: int32 [32], replicated, may hold values from 0 to 4095
Outputs:
- stacks: float32 [32, 2, 61, 4096], P('tm', None, None, 'recv')
All inputs are finite; a program needn't handle non-finite values. No bound on the sum of `valid` on one device may be relied on, other than what follows from the above.
Results may differ from a plain program's by a relative error of at most 0.0035.
Values sent between devices are 32-bit elements; how exact they have to be, the bound alone decides.
No kernel may reach another device: no remote copies, remote signals or barrier semaphores. Data moves between devices by JAX's collectives and lax.ppermute only.
A program may use at most 64 MiB of HBM per device.

v0:
```python
import math
import jax
import jax.numpy as jnp
from jax import lax
from jax.sharding import PartitionSpec as P

NS = 2048
NB = 61
BIN0 = 40


def basis_table():
    sample_ids = jnp.arange(NS, dtype=jnp.int32)
    bin_ids = BIN0 + jnp.arange(NB, dtype=jnp.int32)
    phase_ids = bin_ids[:, None] * sample_ids[None, :] % NS
    angle = 2.0 * math.pi / NS * phase_ids.astype(jnp.float32)
    return jnp.concatenate([jnp.cos(angle), -jnp.sin(angle)], axis=0).astype(jnp.bfloat16)


def whiten_block(spec, valid_float):
    real_part = spec[:NB]
    imag_part = spec[NB:]
    power = real_part * real_part + imag_part * imag_part
    level = jnp.sum(power, axis=0) / (2.0 * NB)
    scale = lax.rsqrt(power + level[None] + 1e-06) * valid_float[None]
    return jnp.concatenate([real_part * scale, imag_part * scale], axis=0)


def share_panel(partial_value):
    return lax.psum(partial_value, "recv")


def cross_terms(panel, white, factor):
    high = lax.Precision.HIGHEST
    src_real = panel[:NB]
    src_imag = panel[NB:]
    own_real = white[:NB]
    own_imag = white[NB:]
    real_sum = jnp.einsum("fts,ftc->sfc", src_real, own_real, precision=high) + jnp.einsum(
        "fts,ftc->sfc", src_imag, own_imag, precision=high
    )
    imag_sum = jnp.einsum("fts,ftc->sfc", src_real, own_imag, precision=high) - jnp.einsum(
        "fts,ftc->sfc", src_imag, own_real, precision=high
    )
    return jnp.stack([real_sum, imag_sum], axis=1) * factor


def on_device(traces, valid, src_idx):
    seg_count = traces.shape[0]
    chan_count = traces.shape[1]
    basis = basis_table()
    valid_float = valid.astype(jnp.float32)
    offset = lax.axis_index("recv") * chan_count
    onehot = (src_idx[:, None] == offset + jnp.arange(chan_count, dtype=jnp.int32)[None, :]).astype(
        jnp.float32
    )
    spec = lax.dot_general(
        basis, traces, (((1,), (2,)), ((), ())), preferred_element_type=jnp.float32
    )
    white = whiten_block(spec, valid_float)
    partial_value = jnp.einsum("ktc,sc->kts", white, onehot, precision=lax.Precision.HIGHEST)
    panel = share_panel(partial_value)
    factor = 1.0 / math.sqrt(seg_count * lax.axis_size("tm"))
    totals = cross_terms(panel, white, factor)
    return lax.psum_scatter(totals, "tm", scatter_dimension=0, tiled=True)


def solution(mesh):
    return jax.shard_map(
        on_device,
        mesh=mesh,
        in_specs=(P("tm", "recv", None), P("tm", "recv"), P()),
        out_specs=P("tm", None, None, "recv"),
        check_vma=False,
    )
```

profile of v0, /device:TPU:2, one launch (start us, length us, event | category | flops | bytes accessed | tf_op | source)
XLA Modules:
  0.0 392.3 jit_solution(107525465795028076)
XLA Ops:
  6.5 0.0 all-reduce.3.cloned.1.call-start
  6.5 2.4 cosine_convert_fusion
  9.0 0.0 copy-start
  9.0 0.0 copy-start.1
  9.0 3.7 fusion.3
  12.7 0.1 fusion.25
  12.8 0.0 copy-done
  12.9 0.1 slice_multiply_fusion.1
  13.0 0.0 copy-done.1
  13.0 0.4 fusion.6
  13.4 68.9 %psum.7 = f32[122,4,32]{0,2,1:T(8,128)S(1)} all-reduce(f32[122,4,32]{0,2,1:T(8,128)S(1)} %fusion.6), channel_id=1, replica_groups=mesh['tm'=32,'recv'=16] {'recv'}, use_global_device_ids=true, to_apply=%region_1.2 | all-reduce | flops 15616 | bytes 124928 | tf_op jit(solution)/shard_map/psum | solution.py:30
  82.3 0.1 fusion.26
  82.4 0.1 copy.14
  82.5 3.1 fusion.17
  85.6 1.8 fusion.13
  87.4 0.1 copy.16
  87.5 3.3 add_bitcast_fusion
  90.8 1.8 subtract_bitcast_fusion
  92.6 0.5 maximum_multiply_fusion
  93.1 5.0 %copy.21 = f32[32,2,61,256]{3,1,2,0:T(2,128)} copy(f32[32,2,61,256]{3,0,2,1:T(8,128)S(1)} %maximum_multiply_fusion) | data formatting | bytes 7995392 | tf_op jit(solution)/shard_map/mul | solution.py:45
  98.1 0.0 all-reduce.3.cloned.1.call-update
  98.1 1.2 dynamic-slice
  99.3 284.0 %all-reduce.3.cloned.1.call-done = f32[32,2,61,256]{3,1,2,0:T(2,128)} async-done(((f32[32,2,61,256]{3,1,2,0:T(2,128)}), f32[32,2,61,256]{3,1,2,0:T(2,128)}) %all-reduce.3.cloned.1.call-update) | async-done | bytes 3997712
  383.4 2.1 constant_dynamic-slice_fusion
  (4 shorter events, 0.0 us)
Async XLA Ops:
  6.5 376.8 %all-reduce.3.cloned.1.call-start = ((), (), s32[]{:S(2)}) async-start(), calls=%async_computation | async-start | bytes 7995392
  9.0 3.8 copy-start
  9.0 4.0 %copy-start.1 = (s32[32]{0:T(128)S(1)}, s32[32]{0:T(128)}, u32[]{:S(2)}) copy-start(s32[32]{0:T(128)} %param.5) | copy-start | bytes 388
Sparse Core Ops, SparseCore 0:
  98.2 285.1 all-reduce.2
where the time goes:
time: 393 us; the launch traced here: 392 us
  waiting for transfers between devices  284 us (72%)
  blocking collectives  68.9 us (18%)
  matrix products  14.1 us (4%)
  between operations  13.5 us (3%)
  local copies, waits for them, and re-layouts  8.66 us (2%)
    unnamed x2, waiting for transfers between devices  284 us
    psum x1, blocking collectives, share_panel(): return lax.psum(partial_value, 'recv')  68.9 us
  transfers between devices with their start and end apart: 1, of which 1 were waited for; matrix products, arithmetic and copies ran while one was open for 0% of the time, Pallas kernels for 0%

commit v1 on v0

--- a/solution.py
+++ b/solution.py
@@ -27,7 +27,12 @@
 
 
 def share_panel(partial_value):
-    return lax.psum(partial_value, "recv")
+
+    def save_results(state, named_axis):
+        x_new = jnp.sum(lax.all_gather(state, named_axis), axis=0)
+        return x_new
+
+    return save_results(partial_value, "recv")
 
 
 def cross_terms(panel, white, factor):

time: 393 us -> 362 us (0.921)
  blocking collectives: 68.9 us -> 38.9 us
    psum x1 -> x0, blocking collectives: 68.9 us -> none  [share_panel(): return lax.psum(partial_value, 'recv')]
    all_gather x0 -> x1, blocking collectives: none -> 38.9 us  [save_results(): x_new = jnp.sum(lax.all_gather(state, named_axis), axis=0)]
where the time goes in v1:
time: 362 us
  waiting for transfers between devices  283 us (78%)
  blocking collectives  38.9 us (11%)
  between operations  13.5 us (4%)
  matrix products  11.2 us (3%)
  local copies, waits for them, and re-layouts  8.49 us (2%)
  other arithmetic  6.11 us (2%)
    unnamed x2, waiting for transfers between devices  283 us
    all_gather x1, blocking collectives, save_results(): x_new = jnp.sum(lax.all_gather(state, named_axis), axis=0)  38.9 us
  transfers between devices with their start and end apart: 1, of which 1 were waited for; matrix products, arithmetic and copies ran while one was open for 0% of the time, Pallas kernels for 0%

profile of v1, /device:TPU:2, one launch (start us, length us, event | category | flops | bytes accessed | tf_op | source)
XLA Modules:
  0.0 361.6 jit_solution(8717010030322363761)
XLA Ops:
  6.5 0.0 copy-start
  6.5 0.0 copy-start.1
  6.5 0.0 all-reduce.3.cloned.1.call-start
  6.6 2.5 cosine_convert_fusion
  9.0 3.7 %fusion.3 = f32[122,4,256]{2,0,1:T(8,128)S(1)} fusion(bf16[4,256,2048]{2,1,0:T(8,128)(2,1)} %param.3, bf16[61,2048]{1,0:T(8,128)(2,1)S(1)} %get-tuple-element.8, bf16[61,2048]{1,0:T(8,128)(2,1)S(1)} %get-tuple-element.7), kind=kOutput, calls=%fused_computation.10 | convolution fusion | flops 512704512 | bytes 5193728 | tf_op jit(solution)/shard_map/dot_general | solution.py:62
  12.7 0.1 fusion.29
  12.8 0.0 copy-done
  12.8 0.1 slice_multiply_fusion.1
  13.0 0.0 copy-done.1
  13.0 0.4 fusion.6
  13.4 0.2 copy.9
  13.5 38.9 %all-gather = f32[1952,4,32]{2,1,0:T(4,128)} all-gather(f32[122,4,32]{2,1,0:T(4,128)S(1)} %copy.9), channel_id=2, replica_groups=mesh['tm'=32,'recv'=16] {'recv'}, dimensions={0}, use_global_device_ids=true | all-gather | bytes 1061888 | tf_op jit(solution)/shard_map/all_gather | solution.py:32
  52.4 3.0 reduce_sum.19
  55.4 1.8 fusion.17
  57.2 1.8 fusion.13
  59.0 1.8 add_bitcast_fusion
  60.8 1.8 subtract_bitcast_fusion
  62.6 0.5 maximum_multiply_fusion
  63.1 5.0 %copy.17 = f32[32,2,61,256]{3,1,2,0:T(2,128)} copy(f32[32,2,61,256]{3,0,2,1:T(8,128)S(1)} %maximum_multiply_fusion) | data formatting | bytes 7995392 | tf_op jit(solution)/shard_map/mul | solution.py:50
  68.0 0.0 all-reduce.3.cloned.1.call-update
  68.1 1.2 dynamic-slice
  69.3 283.4 %all-reduce.3.cloned.1.call-done = f32[32,2,61,256]{3,1,2,0:T(2,128)} async-done(((f32[32,2,61,256]{3,1,2,0:T(2,128)}), f32[32,2,61,256]{3,1,2,0:T(2,128)}) %all-reduce.3.cloned.1.call-update) | async-done | bytes 3997712
  352.7 2.1 constant_dynamic-slice_fusion
  (4 shorter events, 0.0 us)
Async XLA Ops:
  6.5 6.3 %copy-start = (s32[4,256]{1,0:T(4,128)S(1)}, s32[4,256]{1,0:T(4,128)}, u32[]{:S(2)}) copy-start(s32[4,256]{1,0:T(4,128)} %param.4) | copy-start | bytes 12292
  6.5 6.4 %copy-start.1 = (s32[32]{0:T(128)S(1)}, s32[32]{0:T(128)}, u32[]{:S(2)}) copy-start(s32[32]{0:T(128)} %param.5) | copy-start | bytes 388
  6.5 346.1 %all-reduce.3.cloned.1.call-start = ((), (), s32[]{:S(2)}) async-start(), calls=%async_computation | async-start | bytes 7995392
Sparse Core Ops, SparseCore 0:
  68.2 284.4 all-reduce.2
